TPU v7x, 256 devices: a whole 4x4x8 slice. The times are simulated.
256 devices in a mesh: dp: 32 (over y, z), tensor: 8 (over x, core).
Axes of the slice: x: 4, y: 4, z: 8, core: 2. Of those that a mesh axis runs over, the one named last changes fastest.
Arguments:
- residual_in: bfloat16 [2048, 2048], P(('dp', 'tensor')), may hold values from -6 to 6
- attn_gain: float32 [2048], replicated, may hold values from 0.5 to 1.5
- query_weight: bfloat16 [2048, 4096], P(None, 'tensor'), may hold values from -0.125 to 0.125
- kv_weight: bfloat16 [2048, 1024], P(None, 'tensor'), may hold values from -0.125 to 0.125
- query_gain: float32 [128], replicated, may hold values from 0.25 to 1.75
- key_gain: float32 [128], replicated, may hold values from 0.25 to 1.75
- out_weight: bfloat16 [4096, 2048], P('tensor'), may hold values from -0.09375 to 0.09375
- moe_gain: float32 [2048], replicated, may hold values from 0.5 to 1.5
- gate_weight: bfloat16 [128, 2048, 768], P('dp', None, 'tensor'), may hold values from -0.1875 to 0.1875
- lift_weight: bfloat16 [128, 2048, 768], P('dp', None, 'tensor'), may hold values from -0.1875 to 0.1875
- down_weight: bfloat16 [128, 768, 2048], P('dp', 'tensor'), may hold values from -0.21875 to 0.21875
- routes: int32 [2048, 8], P('dp'), may hold values from 0 to 127, as said below
- route_weights: float32 [2048, 8], P('dp'), may hold values from 0.5 to 1
- prefix_cache: bfloat16 [64, 2048, 1024], P('dp', 'tensor'), may hold values from -250 to 250
- suffix_cache: bfloat16 [2048, 128, 1024], P('dp', 'tensor'), may hold values from -250 to 250
- prefix_len: int32 [64], P('dp'), may hold values from 1 to 2048, as said below
- suffix_len: int32 [2048], P('dp'), may hold values from 1 to 128, as said below
- request_group: int32 [2048], P('dp'), may hold values from 0 to 63, as said below
Outputs:
- layer_out: bfloat16 [2048, 2048], P(('dp', 'tensor'))
- new_cache_rows: bfloat16 [2048, 1024], P('dp', 'tensor')
Inputs may be any that keep to these rules, and one draw needn't show every extreme that they name: `routes`: each block of 64 rows (the requests of one index of dp) names 64 of the experts exactly 8 times each and no other expert; one expert is among them in every block. `request_group`: request r belongs to one of the groups (r // 64) * 2 to (r // 64) * 2 + 1. `prefix_len`: some shared prompt has all 2048 slots live. `suffix_len`: some request has all 128 suffix slots live.
All inputs are finite; a program needn't handle non-finite values.
Results may differ from a plain program's by a relative error of at most 0.02.
Values may be sent and summed in bfloat16 or wider, within the bound.
No kernel may reach another device: no remote copies, remote signals or barrier semaphores. Data moves between devices by JAX's collectives and lax.ppermute only.
A program may use at most 128 MiB of HBM per device.

v0:
```python
import math
import jax
import jax.numpy as jnp
from jax import lax
from jax.sharding import PartitionSpec as P

EPSILON = 1e-06
THETA = 1000000.0
NEGATIVE = -1e30


def merged(array, axis, combine):
    everything = jax.tree.map(lambda part: lax.all_gather(part, axis), array)
    first = jax.tree.map(lambda part: part[0], everything)

    def hop(k, so_far):
        return combine(so_far, jax.tree.map(lambda part: part[k], everything))

    return lax.fori_loop(1, lax.axis_size(axis), hop, first)


def rms_scale(values, gain):
    mean_square = jnp.mean(values * values, axis=-1, keepdims=True)
    return values * lax.rsqrt(mean_square + EPSILON) * gain


def rotate(values, positions):
    half = values.shape[-1] // 2
    freqs = THETA ** (-jnp.arange(half).astype(jnp.float32) * 2.0 / values.shape[-1])
    angles = positions.astype(jnp.float32)[:, None] * freqs[None, :]
    angles = jnp.concatenate([angles, angles], axis=-1)
    cosine = jnp.cos(angles)[:, None, :]
    sine = jnp.sin(angles)[:, None, :]
    turned = jnp.concatenate([-values[..., half:], values[..., :half]], axis=-1)
    return values * cosine + turned * sine


def combine_parts(first, second):
    top_first, total_first, sums_first = first
    top_second, total_second, sums_second = second
    top_new = jnp.maximum(top_first, top_second)
    factor_first = jnp.exp(top_first - top_new)
    factor_second = jnp.exp(top_second - top_new)
    return (
        top_new,
        total_first * factor_first + total_second * factor_second,
        sums_first * factor_first[..., None] + sums_second * factor_second[..., None],
    )


def body(
    residual_in,
    attn_gain,
    query_weight,
    kv_weight,
    query_gain,
    key_gain,
    out_weight,
    moe_gain,
    gate_weight,
    lift_weight,
    down_weight,
    routes,
    route_weights,
    prefix_cache,
    suffix_cache,
    prefix_len,
    suffix_len,
    request_group,
):
    tensor_size = lax.axis_size("tensor")
    tensor_rank = lax.axis_index("tensor")
    dp_rank = lax.axis_index("dp")
    owners = lax.axis_size("dp")
    head_dim = query_gain.shape[0]
    requests = routes.shape[0]
    model_width = residual_in.shape[1]
    query_cols = query_weight.shape[1]
    kv_cols = kv_weight.shape[1]
    heads_here = query_cols // head_dim
    heads_all = heads_here * tensor_size
    kv_heads_all = kv_cols * tensor_size // (2 * head_dim)
    per_group = heads_all // kv_heads_all
    groups_dev = prefix_cache.shape[0]
    pre_local = prefix_cache.shape[1]
    suf_local = suffix_cache.shape[1]
    normed = rms_scale(residual_in.astype(jnp.float32), attn_gain).astype(jnp.bfloat16)
    piece = lax.all_gather(normed, "tensor", axis=0, tiled=True)
    projected = jnp.concatenate(
        [
            jnp.dot(piece, query_weight, preferred_element_type=jnp.float32),
            jnp.dot(piece, kv_weight, preferred_element_type=jnp.float32),
        ],
        axis=1,
    )
    query_raw = projected[:, :query_cols].reshape(requests, heads_here, head_dim)
    kv_raw = projected[:, query_cols:].reshape(requests, kv_cols // head_dim, head_dim)
    group_ids = dp_rank * groups_dev + jnp.arange(groups_dev)
    member = request_group[:, None] == group_ids[None, :]
    prefix_of = jnp.sum(jnp.where(member, prefix_len[None, :], 0), axis=1)
    positions = prefix_of + suffix_len
    queries = rotate(rms_scale(query_raw, query_gain), positions).astype(jnp.bfloat16)
    head_number = tensor_rank * (kv_cols // head_dim) + jnp.arange(kv_cols // head_dim)
    is_key = (head_number < kv_heads_all)[None, :, None]
    keyed = rotate(rms_scale(kv_raw, key_gain), positions)
    new_rows = jnp.where(is_key, keyed, kv_raw).astype(jnp.bfloat16).reshape(requests, kv_cols)
    joined = jnp.concatenate([queries.reshape(requests, query_cols), new_rows], axis=1)
    every_head = lax.all_gather(joined, "tensor", axis=1, tiled=True).reshape(
        requests, tensor_size, query_cols + kv_cols
    )
    all_queries = every_head[:, :, :query_cols].reshape(requests, kv_heads_all, per_group, head_dim)
    all_kv = every_head[:, :, query_cols:]
    own_keys = all_kv[:, :kv_heads_all]
    own_values = all_kv[:, kv_heads_all:].astype(jnp.float32)
    scale = 1.0 / math.sqrt(head_dim)
    split_at = kv_heads_all * head_dim
    pre_keys = prefix_cache[:, :, :split_at].reshape(groups_dev, pre_local, kv_heads_all, head_dim)
    pre_values = prefix_cache[:, :, split_at:].reshape(
        groups_dev, pre_local, kv_heads_all, head_dim
    )
    suf_keys = suffix_cache[:, :, :split_at].reshape(requests, suf_local, kv_heads_all, head_dim)
    suf_values = suffix_cache[:, :, split_at:].reshape(requests, suf_local, kv_heads_all, head_dim)
    pre_scores = (
        jnp.einsum("rgqd,npgd->rgqnp", all_queries, pre_keys, preferred_element_type=jnp.float32)
        * scale
    )
    suf_scores = (
        jnp.einsum("rgqd,rsgd->rgqs", all_queries, suf_keys, preferred_element_type=jnp.float32)
        * scale
    )
    own_scores = (
        jnp.einsum("rgqd,rgd->rgq", all_queries, own_keys, preferred_element_type=jnp.float32)
        * scale
    )
    pre_slots = tensor_rank * pre_local + jnp.arange(pre_local)
    pre_valid = (member[:, :, None] & (pre_slots[None, None, :] < prefix_len[None, :, None]))[
        :, None, None, :, :
    ]
    suf_slots = tensor_rank * suf_local + jnp.arange(suf_local)
    suf_valid = (suf_slots[None, :] < suffix_len[:, None])[:, None, None, :]
    own_valid = tensor_rank == 0
    top_pre = jnp.max(jnp.where(pre_valid, pre_scores, NEGATIVE), axis=(3, 4))
    top_suf = jnp.max(jnp.where(suf_valid, suf_scores, NEGATIVE), axis=3)
    top_own = jnp.where(own_valid, own_scores, NEGATIVE)
    top_local = jnp.maximum(jnp.maximum(top_pre, top_suf), top_own)
    pre_weights = jnp.where(pre_valid, jnp.exp(pre_scores - top_local[..., None, None]), 0.0)
    suf_weights = jnp.where(suf_valid, jnp.exp(suf_scores - top_local[..., None]), 0.0)
    own_weights = jnp.where(own_valid, jnp.exp(own_scores - top_local), 0.0)
    total_local = jnp.sum(pre_weights, axis=(3, 4)) + jnp.sum(suf_weights, axis=3) + own_weights
    sums_local = jnp.einsum(
        "rgqnp,npgd->rgqd",
        pre_weights.astype(jnp.bfloat16),
        pre_values,
        preferred_element_type=jnp.float32,
    )
    sums_local = sums_local + jnp.einsum(
        "rgqs,rsgd->rgqd",
        suf_weights.astype(jnp.bfloat16),
        suf_values,
        preferred_element_type=jnp.float32,
    )
    own_low = own_weights.astype(jnp.bfloat16).astype(jnp.float32)
    sums_local = sums_local + own_low[..., None] * own_values[:, :, None, :]
    top_local = top_local.reshape(requests, heads_all)
    total_local = total_local.reshape(requests, heads_all)
    sums_local = sums_local.reshape(requests, heads_all, head_dim)
    top_all, total_all, sums_all = merged(
        (top_local, total_local, sums_local), "tensor", combine_parts
    )
    total_mine = lax.dynamic_slice_in_dim(total_all, tensor_rank * heads_here, heads_here, 1)
    sums_mine = lax.dynamic_slice_in_dim(sums_all, tensor_rank * heads_here, heads_here, 1)
    mixed = sums_mine / total_mine[..., None]
    attn_heads = mixed.reshape(requests, query_cols).astype(jnp.bfloat16)
    attn_out = lax.psum_scatter(
        jnp.dot(attn_heads, out_weight, preferred_element_type=jnp.float32).astype(jnp.bfloat16),
        "tensor",
        scatter_dimension=0,
        tiled=True,
    ).astype(jnp.float32)
    middle = (residual_in.astype(jnp.float32) + attn_out).astype(jnp.bfloat16)
    moe_in = rms_scale(middle.astype(jnp.float32), moe_gain).astype(jnp.bfloat16)
    local_experts = gate_weight.shape[0]
    experts_all = local_experts * owners
    topk = routes.shape[1]
    capacity = 2 * requests * topk // experts_all
    flat_routes = routes.reshape(-1)
    onehot = (flat_routes[:, None] == jnp.arange(experts_all)[None, :]).astype(jnp.int32)
    running = jnp.cumsum(onehot, axis=0)
    slot_of = jnp.sum(onehot * running, axis=1) - 1
    code_of = (flat_routes * capacity + slot_of).reshape(requests, topk)
    code_span = jnp.arange(experts_all * capacity)
    placing = jnp.any(code_of[None, :, :] == code_span[:, None, None], axis=2).astype(jnp.bfloat16)
    share = route_weights / jnp.sum(route_weights, axis=1, keepdims=True)
    placed = jnp.dot(
        placing,
        lax.all_gather(moe_in, "tensor", axis=0, tiled=True),
        preferred_element_type=jnp.float32,
    )
    outgoing = placed.astype(jnp.bfloat16).reshape(owners, local_experts, capacity, model_width)
    rows = lax.all_to_all(outgoing, "dp", split_axis=0, concat_axis=0, tiled=True)
    gate_val = jnp.einsum("necd,edf->necf", rows, gate_weight, preferred_element_type=jnp.float32)
    lift_val = jnp.einsum("necd,edf->necf", rows, lift_weight, preferred_element_type=jnp.float32)
    hidden_units = (jax.nn.silu(gate_val) * lift_val).astype(jnp.bfloat16)
    returned = lax.all_to_all(
        jnp.einsum(
            "necf,efd->necd", hidden_units, down_weight, preferred_element_type=jnp.float32
        ).astype(jnp.bfloat16),
        "dp",
        split_axis=0,
        concat_axis=0,
        tiled=True,
    ).astype(jnp.float32)
    returned = returned.reshape(experts_all * capacity, model_width)
    picked_rows = returned[code_of]
    moe_out = lax.psum_scatter(
        jnp.sum(share[:, :, None] * picked_rows, axis=1).astype(jnp.bfloat16),
        "tensor",
        scatter_dimension=0,
        tiled=True,
    ).astype(jnp.float32)
    layer_out = (middle.astype(jnp.float32) + moe_out).astype(jnp.bfloat16)
    return (layer_out, new_rows)


def solution(mesh):
    in_specs = (
        P(("dp", "tensor"), None),
        P(),
        P(None, "tensor"),
        P(None, "tensor"),
        P(),
        P(),
        P("tensor", None),
        P(),
        P("dp", None, "tensor"),
        P("dp", None, "tensor"),
        P("dp", "tensor", None),
        P("dp", None),
        P("dp", None),
        P("dp", "tensor", None),
        P("dp", "tensor", None),
        P("dp"),
        P("dp"),
        P("dp"),
    )
    out_specs = (P(("dp", "tensor"), None), P("dp", "tensor"))
    return jax.shard_map(body, mesh=mesh, in_specs=in_specs, out_specs=out_specs, check_vma=False)
```

profile of v0, /device:TPU:8, one launch (start us, length us, event | category | flops | bytes accessed | tf_op | source)
XLA Modules:
  0.0 472.5 jit_solution(8575406757492180028)
XLA Ops:
  7.3 1.0 fusion.77
  8.3 0.8 fusion.79
  9.2 13.2 %all_gather.18 = bf16[64,2048]{1,0:T(8,128)(2,1)S(1)} all-gather(bf16[8,2048]{1,0:T(8,128)(2,1)S(1)} %fusion.79), channel_id=1, replica_groups=mesh['dp'=32,'tensor'=8] {'tensor'}, dimensions={0}, use_global_device_ids=true | all-gather | bytes 294912 | tf_op jit(solution)/shard_map/all_gather | solution.py:88
  22.4 1.4 multiply_reduce_fusion.1
  23.7 0.7 fusion.91
  24.6 2.1 fusion.100
  27.2 0.2 select_reduce_fusion.1
  27.4 0.2 fusion.93
  28.0 13.3 %all_gather.19 = bf16[64,5120]{1,0:T(8,128)(2,1)S(1)} all-gather(bf16[64,640]{1,0:T(8,128)(2,1)S(1)} %pad_maximum_fusion), channel_id=1, replica_groups=mesh['dp'=32,'tensor'=8] {'tensor'}, dimensions={1}, use_global_device_ids=true | all-gather | bytes 737280 | tf_op jit(solution)/shard_map/all_gather | solution.py:108
  41.6 0.3 reshape.299
  42.0 0.4 fusion.75
  42.5 2.1 fusion.98
  44.7 2.0 copy.234
  46.8 4.0 fusion.4
  51.0 3.0 slice_bitcast_fusion.1
  54.0 1.7 select_reduce_fusion
  56.0 1.0 copy.235
  57.2 2.0 fusion.55
  59.2 3.3 fusion.23
  62.5 0.6 fusion.26
  63.2 1.2 copy.292
  64.8 0.2 fusion.69
  65.2 12.8 %all_gather.20 = f32[8,64,32]{1,2,0:T(8,128)S(1)} all-gather(f32[1,64,32]{1,2,0:T(8,128)S(1)} %bitcast.195), channel_id=1, replica_groups=mesh['dp'=32,'tensor'=8] {'tensor'}, dimensions={0}, use_global_device_ids=true | all-gather | bytes 73728 | tf_op jit(solution)/shard_map/all_gather | solution.py:13
  78.0 4.1 fusion.12
  82.3 13.5 %all_gather.21 = f32[8,64,32]{1,2,0:T(8,128)S(1)} all-gather(f32[1,64,32]{1,2,0:T(8,128)S(1)} %add_bitcast_fusion), channel_id=1, replica_groups=mesh['dp'=32,'tensor'=8] {'tensor'}, dimensions={0}, use_global_device_ids=true | all-gather | bytes 73728 | tf_op jit(solution)/shard_map/all_gather | solution.py:13
  95.9 0.8 fusion.67
  96.7 22.8 %all-gather.2.cloned.1.call-done = f32[8,64,32,128]{3,2,1,0:T(8,128)} async-done(((f32[1,64,32,128]{3,2,1,0:T(8,128)}), f32[8,64,32,128]{3,2,1,0:T(8,128)}) %all-gather.2.cloned.1.call-update) | async-done | bytes 8388624 | tf_op jit(solution)/shard_map/all_gather | solution.py:13
  119.5 1.3 slice_bitcast_fusion
  120.9 20.0 %while.19 = (s32[]{:T(128)}, f32[64,32]{1,0:T(8,128)S(1)}, f32[64,32]{1,0:T(8,128)S(1)}, f32[64,32,128]{2,1,0:T(8,128)S(1)}, f32[8,64,32]{1,2,0:T(8,128)S(1)}, /...) while((s32[]{:T(128)}, f32[64,32]{1,0:T(8,128)S(1)}, ...), condition=%wide.region_9.10_spmd, body=%wide.region_8.9_spmd.sunk | while | flops 798725 | bytes 3293335 | solution.py:19
  120.9 0.7 constant_dynamic-slice_fusion.4
  121.8 1.9 fusion.114
  123.7 0.7 constant_dynamic-slice_fusion.4
  124.7 1.9 fusion.114
  126.6 0.7 constant_dynamic-slice_fusion.4
  127.5 1.9 fusion.114
  129.4 0.7 constant_dynamic-slice_fusion.4
  130.4 1.9 fusion.114
  132.3 0.7 constant_dynamic-slice_fusion.4
  133.2 1.9 fusion.114
  135.1 0.7 constant_dynamic-slice_fusion.4
  136.1 1.9 fusion.114
  138.0 0.7 constant_dynamic-slice_fusion.4
  138.9 1.9 fusion.114
  140.9 0.1 fusion.74
  141.1 1.2 convolution_convert_fusion.1
  142.6 0.7 fusion.18
  143.3 32.8 %reduce-scatter.3.cloned.1.call-done = bf16[8,2048]{1,0:T(8,128)(2,1)} async-done(((bf16[64,2048]{1,0:T(8,128)(2,1)}), bf16[8,2048]{1,0:T(8,128)(2,1)}) %reduce-scatter.3.cloned.1.call-update) | async-done | bytes 32784 | tf_op jit(solution)/shard_map/reduce_scatter | solution.py:174
  176.1 0.9 fusion.81
  177.0 0.8 fusion.83
  177.8 12.8 %all_gather.23 = bf16[64,2048]{1,0:T(8,128)(2,1)S(1)} all-gather(bf16[8,2048]{1,0:T(8,128)(2,1)S(1)} %fusion.83), channel_id=1, replica_groups=mesh['dp'=32,'tensor'=8] {'tensor'}, dimensions={0}, use_global_device_ids=true | all-gather | bytes 294912 | tf_op jit(solution)/shard_map/all_gather | solution.py:196
  190.7 1.3 convolution_convert_fusion
  192.0 104.1 %all_to_all.10 = bf16[32,4,8,2048]{3,2,1,0:T(8,128)(2,1)S(1)} all-to-all(bf16[32,4,8,2048]{3,2,1,0:T(8,128)(2,1)S(1)} %bitcast.183), channel_id=1, replica_groups=mesh['dp'=32,'tensor'=8] {'dp'}, dimensions={0} | all-to-all | bytes 8388608 | tf_op jit(solution)/shard_map/all_to_all | solution.py:200
  296.1 2.0 copy-done.2
  298.1 1.2 fusion.27
  299.3 7.4 %convert_bitcast_fusion = bf16[32,4,8,2048]{3,2,0,1:T(8,128)(2,1)} fusion(bf16[4,96,2048]{2,1,0:T(8,128)(2,1)} %param.30, bf16[4,2048,96]{1,2,0:T(8,128)(2,1)} %param.29, bf16[32,4,8,2048]{3,2,1,0:T(8,128)(2,1)} %copy-done.2, f32[32,4,8,96]{3,2,0,1:T(8,128)S(1)} %fusion.27), kind=kOutput, calls=%fused_computation.19 | convolution fusion | flops 807993344 | bytes 11927552 | tf_op jit(solution)/shard_map/necf,efd->necd/dot_general | solution.py:205
  306.7 4.7 %copy.211 = bf16[32,4,8,2048]{3,2,1,0:T(8,128)(2,1)} copy(bf16[32,4,8,2048]{3,2,0,1:T(8,128)(2,1)} %convert_bitcast_fusion) | data formatting | bytes 8388608 | tf_op jit(solution)/shard_map/convert_element_type | solution.py:207
  311.4 7.8 %all-to-all-start.1 = ((bf16[32,4,8,2048]{3,2,1,0:T(8,128)(2,1)}), bf16[32,4,8,2048]{3,2,1,0:T(8,128)(2,1)}, u32[]{:S(2)}, u32[]{:S(2)}) async-start(bf16[32,4,8,2048]{3,2,1,0:T(8,128)(2,1)} %copy.211), calls=%async_computation.2 | async-start | bytes 8388608 | tf_op jit(solution)/shard_map/all_to_all | solution.py:204
  319.2 0.3 reduce-scatter.5.cloned.1.call-start
  319.8 93.7 %all-to-all-done.1 = bf16[32,4,8,2048]{3,2,1,0:T(8,128)(2,1)} async-done(((bf16[32,4,8,2048]{3,2,1,0:T(8,128)(2,1)}), bf16[32,4,8,2048]{3,2,1,0:T(8,128)(2,1)}, u32[]{:S(2)}, u32[]{:S(2)}) %all-to-all-start.1) | async-done | bytes 4194336 | tf_op jit(solution)/shard_map/all_to_all | solution.py:204
  413.5 6.5 %bitcast_convert_fusion = f32[1024,2048]{1,0:T(8,128)} fusion(bf16[32,4,8,2048]{3,2,1,0:T(8,128)(2,1)} %all-to-all-done.1), kind=kLoop, calls=%fused_computation.11 | loop fusion | flops 2097152 | bytes 12582912 | tf_op jit(solution)/shard_map/reshape | solution.py:213
  419.9 8.9 %gather_fusion = f32[512,2048]{1,0:T(8,128)} fusion(f32[1024,2048]{1,0:T(8,128)} %bitcast_convert_fusion, s32[1024]{0:T(1024)S(1)} %pad_clamp_fusion), kind=kCustom, calls=%fused_computation | custom fusion | bytes 8390656 | tf_op jit(solution)/shard_map/gather | solution.py:214
  428.8 4.3 fusion.3
  433.2 31.4 %reduce-scatter.5.cloned.1.call-done = bf16[8,2048]{1,0:T(8,128)(2,1)} async-done(((bf16[64,2048]{1,0:T(8,128)(2,1)}), bf16[8,2048]{1,0:T(8,128)(2,1)}) %reduce-scatter.5.cloned.1.call-update) | async-done | bytes 32784 | tf_op jit(solution)/shard_map/reduce_scatter | solution.py:215
  464.6 1.4 fusion.84
  (132 shorter events, 5.2 us)
Async XLA Ops:
  7.2 133.9 %copy-start = (bf16[512,2048]{1,0:T(8,128)(2,1)S(1)}, bf16[512,2048]{1,0:T(8,128)(2,1)}, u32[]{:S(2)}) copy-start(bf16[512,2048]{1,0:T(8,128)(2,1)} %param.26) | copy-start | bytes 6291460
  7.2 20.3 %copy-start.15 = (f32[128]{0:T(128)S(1)}, f32[128]{0:T(128)}, u32[]{:S(2)}) copy-start(f32[128]{0:T(128)} %param.25) | copy-start | bytes 1540
  7.2 19.7 %copy-start.16 = (f32[128]{0:T(128)S(1)}, f32[128]{0:T(128)}, u32[]{:S(2)}) copy-start(f32[128]{0:T(128)} %param.24) | copy-start | bytes 1540
  7.2 20.0 %copy-start.18 = (s32[2]{0:T(128)S(1)}, s32[2]{0:T(128)}, u32[]{:S(2)}) copy-start(s32[2]{0:T(128)} %param.35) | copy-start | bytes 28
  7.2 20.0 %copy-start.17 = (s32[64]{0:T(128)S(1)}, s32[64]{0:T(128)}, u32[]{:S(2)}) copy-start(s32[64]{0:T(128)} %param.37) | copy-start | bytes 772
  7.2 20.1 %copy-start.19 = (s32[64]{0:T(128)S(1)}, s32[64]{0:T(128)}, u32[]{:S(2)}) copy-start(s32[64]{0:T(128)} %param.36) | copy-start | bytes 772
  7.2 112.3 %all-gather.2.cloned.1.call-start = ((), (), s32[]{:S(2)}) async-start(), calls=%async_computation.4 | async-start | bytes 9437184 | tf_op jit(solution)/shard_map/all_gather | solution.py:13
  27.7 13.7 %copy-start.9 = (bf16[64,128]{1,0:T(8,128)(2,1)}, bf16[64,128]{1,0:T(8,128)(2,1)S(1)}, u32[]{:S(2)}) copy-start(bf16[64,128]{1,0:T(8,128)(2,1)S(1)} %get-tuple-element.258) | copy-start | bytes 49156
  42.5 13.3 %copy-start.7 = (f32[64,4,1,8]{0,3,1,2:T(8,128)}, f32[64,4,1,8]{0,3,1,2:T(8,128)S(1)}, u32[]{:S(2)}) copy-start(f32[64,4,1,8]{0,3,1,2:T(8,128)S(1)} %copy.216) | copy-start | bytes 24580
  57.1 5.4 %copy-start.3 = (bf16[64,2,4,8,128]{4,3,2,1,0:T(8,128)(2,1)S(1)}, bf16[64,2,4,8,128]{4,3,2,1,0:T(8,128)(2,1)}, u32[]{:S(2)}) copy-start(bf16[64,2,4,8,128]{4,3,2,1,0:T(8,128)(2,1)} %get-tuple-element.247) | copy-start | bytes 3145732
  62.5 1.9 copy-start.11
  64.4 17.9 %copy-start.8 = (f32[64,4,1,8]{0,3,1,2:T(8,128)S(1)}, f32[64,4,1,8]{0,3,1,2:T(8,128)}, u32[]{:S(2)}) copy-start(f32[64,4,1,8]{0,3,1,2:T(8,128)} %copy-done.7) | copy-start | bytes 24580
  64.4 111.7 %reduce-scatter.3.cloned.1.call-start = ((), (), s32[]{:S(2)}) async-start(), calls=%async_computation.5 | async-start | bytes 294912 | tf_op jit(solution)/shard_map/reduce_scatter | solution.py:174
  95.8 25.0 %copy-start.5 = (f32[8,64,32]{1,2,0:T(8,128)}, f32[8,64,32]{1,2,0:T(8,128)S(1)}, u32[]{:S(2)}) copy-start(f32[8,64,32]{1,2,0:T(8,128)S(1)} %all_gather.21) | copy-start | bytes 196612
  120.8 21.5 %copy-start.13 = (s32[512]{0:T(512)S(1)}, s32[512]{0:T(512)}, u32[]{:S(2)}) copy-start(s32[512]{0:T(512)} %fusion.67) | copy-start | bytes 6148
  120.8 21.6 %copy-start.12 = (s32[64,8]{0,1:T(8,128)S(1)}, s32[64,8]{0,1:T(8,128)}, u32[]{:S(2)}) copy-start(s32[64,8]{0,1:T(8,128)} %param.31) | copy-start | bytes 6148
  120.8 55.3 %copy-start.4 = (bf16[8,2048]{1,0:T(8,128)(2,1)S(1)}, bf16[8,2048]{1,0:T(8,128)(2,1)}, u32[]{:S(2)}) copy-start(bf16[8,2048]{1,0:T(8,128)(2,1)} %param.20) | copy-start | bytes 98308
  120.8 56.2 %copy-start.14 = (f32[2048]{0:T(1024)S(1)}, f32[2048]{0:T(1024)}, u32[]{:S(2)}) copy-start(f32[2048]{0:T(1024)} %param.27) | copy-start | bytes 24580
  192.0 106.1 %copy-start.20 = (bf16[4,2048,96]{1,2,0:T(8,128)(2,1)S(1)}, bf16[4,2048,96]{1,2,0:T(8,128)(2,1)}, u32[]{:S(2)}) copy-start(bf16[4,2048,96]{1,2,0:T(8,128)(2,1)} %param.28) | copy-start | bytes 4718596
  296.1 2.0 copy-start.2
  311.4 8.2 %copy-start.10 = (f32[64,8]{0,1:T(8,128)S(1)}, f32[64,8]{0,1:T(8,128)}, u32[]{:S(2)}) copy-start(f32[64,8]{0,1:T(8,128)} %param.32) | copy-start | bytes 6148
  311.4 102.0 %all-to-all-start.1 = ((bf16[32,4,8,2048]{3,2,1,0:T(8,128)(2,1)}), bf16[32,4,8,2048]{3,2,1,0:T(8,128)(2,1)}, u32[]{:S(2)}, u32[]{:S(2)}) async-start(bf16[32,4,8,2048]{3,2,1,0:T(8,128)(2,1)} %copy.211), calls=%async_computation.2 | async-start | bytes 8388608 | tf_op jit(solution)/shard_map/all_to_all | solution.py:204
  319.2 145.4 %reduce-scatter.5.cloned.1.call-start = ((), (), s32[]{:S(2)}) async-start(), calls=%async_computation.6 | async-start | bytes 294912 | tf_op jit(solution)/shard_map/reduce_scatter | solution.py:215
  419.9 46.1 %copy-start.1 = (bf16[512,2048]{1,0:T(8,128)(2,1)S(1)}, bf16[512,2048]{1,0:T(8,128)(2,1)}, u32[]{:S(2)}) copy-start(bf16[512,2048]{1,0:T(8,128)(2,1)} %param.26) | copy-start | bytes 6291460
  428.8 35.8 %copy-start.6 = (bf16[8,2048]{1,0:T(8,128)(2,1)S(1)}, bf16[8,2048]{1,0:T(8,128)(2,1)}, u32[]{:S(2)}) copy-start(bf16[8,2048]{1,0:T(8,128)(2,1)} %reduce-scatter.3.cloned.1.call-done) | copy-start | bytes 98308
Sparse Core Ops, SparseCore 0:
  64.5 54.9 all-gather.1
  142.4 33.6 reduce-scatter.2
  433.3 31.2 reduce-scatter.4
where the time goes:
time: 474 us; the launch traced here: 473 us
  waiting for transfers between devices  181 us (38%)
  blocking collectives  170 us (36%)
  other arithmetic  39.7 us (8%)
  local copies, waits for them, and re-layouts  35.1 us (7%)
  matrix products  24.6 us (5%)
  between operations  14.3 us (3%)
  starting transfers between devices  8.12 us (2%)
    all_to_all x1, blocking collectives, body(): lax.all_to_all(outgoing, 'dp', split_axis=0, concat_axis=0, tiled=True)  104 us
    all_to_all x1, waiting for transfers between devices, body(): lax.all_to_all(jnp.einsum('necf,efd->necd', hidden_units, down_weight, pr...  93.7 us
    reduce_scatter x1, waiting for transfers between devices, body(): lax.psum_scatter(jnp.dot(attn_heads, out_weight, preferred_element_type=j...  32.8 us
    reduce_scatter x1, waiting for transfers between devices, body(): lax.psum_scatter(jnp.sum(share[:, :, None] * picked_rows, axis=1).astype(...  31.4 us
    all_gather x2, blocking collectives, merged(): everything = jax.tree.map(lambda part: lax.all_gather(part, axis), array)  26.3 us
    all_gather x1, waiting for transfers between devices, merged(): everything = jax.tree.map(lambda part: lax.all_gather(part, axis), array)  22.8 us
    all_gather x1, blocking collectives, body(): lax.all_gather(joined, 'tensor', axis=1, tiled=True)  13.3 us
    add x7, other arithmetic, combine_parts(): sums_first * factor_first[..., None]  13.3 us
  transfers between devices with their start and end apart: 4, of which 4 were waited for; matrix products, arithmetic and copies ran while one was open for 2% of the time, Pallas kernels for 0%

commit v1 on v0

--- a/solution.py
+++ b/solution.py
@@ -193,7 +193,9 @@
     share = route_weights / jnp.sum(route_weights, axis=1, keepdims=True)
     placed = jnp.dot(
         placing,
-        lax.all_gather(moe_in, "tensor", axis=0, tiled=True),
+        jnp.concatenate(
+            lax.all_to_all(jnp.stack([moe_in] * lax.axis_size("tensor")), "tensor", 0, 0), axis=0
+        ),
         preferred_element_type=jnp.float32,
     )
     outgoing = placed.astype(jnp.bfloat16).reshape(owners, local_experts, capacity, model_width)

time: 474 us -> 471 us (level)
  blocking collectives: 170 us -> 156 us
    all_gather x1 -> x0, blocking collectives: 12.8 us -> none  [body(): lax.all_gather(moe_in, 'tensor', axis=0, tiled=True)]
    all_to_all x0 -> x1, waiting for transfers between devices: none -> 6.62 us  [body(): lax.all_to_all(jnp.stack([moe_in] * lax.axis_size('tensor')), 'tensor', 0...]
  transfers between devices with their start and end apart: 4 -> 5, of which waited for: 4 -> 5; matrix products, arithmetic and copies ran while one was open for 2% -> 2% of each run, Pallas kernels for 0% -> 0%
where the time goes in v1:
time: 471 us; the launch traced here: 469 us
  waiting for transfers between devices  184 us (39%)
  blocking collectives  156 us (33%)
  other arithmetic  40 us (8%)
  local copies, waits for them, and re-layouts  38.9 us (8%)
  matrix products  24.6 us (5%)
  between operations  14.3 us (3%)
  starting transfers between devices  11.4 us (2%)
    all_to_all x1, blocking collectives, body(): lax.all_to_all(outgoing, 'dp', split_axis=0, concat_axis=0, tiled=True)  103 us
    all_to_all x1, waiting for transfers between devices, body(): lax.all_to_all(jnp.einsum('necf,efd->necd', hidden_units, down_weight, pr...  92.4 us
    reduce_scatter x1, waiting for transfers between devices, body(): lax.psum_scatter(jnp.dot(attn_heads, out_weight, preferred_element_type=j...  32.1 us
    reduce_scatter x1, waiting for transfers between devices, body(): lax.psum_scatter(jnp.sum(share[:, :, None] * picked_rows, axis=1).astype(...  31.6 us
    all_gather x2, blocking collectives, merged(): everything = jax.tree.map(lambda part: lax.all_gather(part, axis), array)  26.3 us
    all_gather x1, waiting for transfers between devices, merged(): everything = jax.tree.map(lambda part: lax.all_gather(part, axis), array)  21 us
    all_gather x1, blocking collectives, body(): lax.all_gather(joined, 'tensor', axis=1, tiled=True)  13.3 us
    add x7, other arithmetic, combine_parts(): sums_first * factor_first[..., None]  13.3 us
  transfers between devices with their start and end apart: 5, of which 5 were waited for; matrix products, arithmetic and copies ran while one was open for 2% of the time, Pallas kernels for 0%

profile of v1, /device:TPU:8, one launch (start us, length us, event | category | flops | bytes accessed | tf_op | source)
XLA Modules:
  0.0 469.5 jit_solution(3126423623912691701)
XLA Ops:
  7.3 1.0 fusion.78
  8.3 0.8 fusion.80
  9.2 13.2 %all_gather.15 = bf16[64,2048]{1,0:T(8,128)(2,1)S(1)} all-gather(bf16[8,2048]{1,0:T(8,128)(2,1)S(1)} %fusion.80), channel_id=1, replica_groups=mesh['dp'=32,'tensor'=8] {'tensor'}, dimensions={0}, use_global_device_ids=true | all-gather | bytes 294912 | tf_op jit(solution)/shard_map/all_gather | solution.py:88
  22.4 1.4 multiply_reduce_fusion.1
  23.7 0.7 fusion.92
  24.6 2.1 fusion.101
  28.0 13.3 %all_gather.16 = bf16[64,5120]{1,0:T(8,128)(2,1)S(1)} all-gather(bf16[64,640]{1,0:T(8,128)(2,1)S(1)} %pad_maximum_fusion), channel_id=1, replica_groups=mesh['dp'=32,'tensor'=8] {'tensor'}, dimensions={1}, use_global_device_ids=true | all-gather | bytes 737280 | tf_op jit(solution)/shard_map/all_gather | solution.py:108
  42.5 2.1 fusion.99
  44.7 2.0 copy.234
  46.8 4.0 fusion.4
  51.0 3.0 slice_bitcast_fusion.1
  54.0 1.7 select_reduce_fusion
  56.0 1.0 copy.235
  57.2 2.0 fusion.55
  59.2 3.3 fusion.23
  62.5 0.6 fusion.26
  63.2 1.2 copy.292
  64.6 0.6 eq.62
  65.6 0.5 slice.66
  66.2 12.7 %all_gather.17 = f32[8,64,32]{1,2,0:T(8,128)S(1)} all-gather(f32[1,64,32]{1,2,0:T(8,128)S(1)} %bitcast.197), channel_id=1, replica_groups=mesh['dp'=32,'tensor'=8] {'tensor'}, dimensions={0}, use_global_device_ids=true | all-gather | bytes 73728 | tf_op jit(solution)/shard_map/all_gather | solution.py:13
  78.9 0.6 copy-done.5
  79.7 4.4 fusion.12
  84.2 13.5 %all_gather.18 = f32[8,64,32]{1,2,0:T(8,128)S(1)} all-gather(f32[1,64,32]{1,2,0:T(8,128)S(1)} %add_bitcast_fusion), channel_id=1, replica_groups=mesh['dp'=32,'tensor'=8] {'tensor'}, dimensions={0}, use_global_device_ids=true | all-gather | bytes 73728 | tf_op jit(solution)/shard_map/all_gather | solution.py:13
  97.7 0.7 copy-done.6
  98.5 21.0 %all-gather.2.cloned.1.call-done = f32[8,64,32,128]{3,2,1,0:T(8,128)} async-done(((f32[1,64,32,128]{3,2,1,0:T(8,128)}), f32[8,64,32,128]{3,2,1,0:T(8,128)}) %all-gather.2.cloned.1.call-update) | async-done | bytes 8388624 | tf_op jit(solution)/shard_map/all_gather | solution.py:13
  119.5 1.3 slice_bitcast_fusion
  120.8 20.1 %while.19 = (s32[]{:T(128)}, f32[64,32]{1,0:T(8,128)S(1)}, f32[64,32]{1,0:T(8,128)S(1)}, f32[64,32,128]{2,1,0:T(8,128)S(1)}, f32[8,64,32]{1,2,0:T(8,128)}, /*ind...) while((s32[]{:T(128)}, f32[64,32]{1,0:T(8,128)S(1)}, ...), condition=%wide.region_9.10_spmd, body=%wide.region_8.9_spmd.sunk | while | flops 798725 | bytes 3293335 | solution.py:19
  120.8 0.7 constant_dynamic-slice_fusion.4
  121.8 1.9 fusion.114
  123.7 0.7 constant_dynamic-slice_fusion.4
  124.6 1.9 fusion.114
  126.6 0.7 constant_dynamic-slice_fusion.4
  127.5 1.9 fusion.114
  129.4 0.7 constant_dynamic-slice_fusion.4
  130.4 1.9 fusion.114
  132.3 0.8 constant_dynamic-slice_fusion.4
  133.3 1.9 fusion.114
  135.2 0.7 constant_dynamic-slice_fusion.4
  136.2 1.9 fusion.114
  138.1 0.7 constant_dynamic-slice_fusion.4
  139.0 1.9 fusion.114
  141.2 1.2 convolution_convert_fusion.1
  142.4 0.6 broadcast.241
  143.1 0.9 fusion.67
  144.1 32.1 %reduce-scatter.3.cloned.1.call-done = bf16[8,2048]{1,0:T(8,128)(2,1)} async-done(((bf16[64,2048]{1,0:T(8,128)(2,1)}), bf16[8,2048]{1,0:T(8,128)(2,1)}) %reduce-scatter.3.cloned.1.call-update) | async-done | bytes 32784 | tf_op jit(solution)/shard_map/reduce_scatter | solution.py:174
  176.2 0.9 fusion.82
  177.1 0.8 fusion.84
  178.0 0.7 stack.2
  178.7 3.4 all-to-all-start
  182.2 0.7 fusion.18
  182.9 6.6 %all-to-all-done = bf16[8,8,2048]{2,1,0:T(8,128)(2,1)S(1)} async-done(((bf16[8,8,2048]{2,1,0:T(8,128)(2,1)}), bf16[8,8,2048]{2,1,0:T(8,128)(2,1)S(1)}, u32[]{:S(2)}, u32[]{:S(2)}) %all-to-all-start) | async-done | bytes 262176 | tf_op jit(solution)/shard_map/all_to_all | solution.py:197
  189.5 1.3 convolution_convert_fusion
  190.8 103.4 %all_to_all.15 = bf16[32,4,8,2048]{3,2,1,0:T(8,128)(2,1)S(1)} all-to-all(bf16[32,4,8,2048]{3,2,1,0:T(8,128)(2,1)S(1)} %bitcast.185), channel_id=1, replica_groups=mesh['dp'=32,'tensor'=8] {'dp'}, dimensions={0} | all-to-all | bytes 8388608 | tf_op jit(solution)/shard_map/all_to_all | solution.py:202
  294.2 2.0 copy-done.2
  296.2 1.2 fusion.27
  297.4 7.4 %convert_bitcast_fusion = bf16[32,4,8,2048]{3,2,0,1:T(8,128)(2,1)} fusion(bf16[4,96,2048]{2,1,0:T(8,128)(2,1)} %param.30, bf16[4,2048,96]{1,2,0:T(8,128)(2,1)} %param.29, bf16[32,4,8,2048]{3,2,1,0:T(8,128)(2,1)} %copy-done.2, f32[32,4,8,96]{3,2,0,1:T(8,128)S(1)} %fusion.27), kind=kOutput, calls=%fused_computation.19 | convolution fusion | flops 807993344 | bytes 11927552 | tf_op jit(solution)/shard_map/necf,efd->necd/dot_general | solution.py:207
  304.8 4.7 %copy.211 = bf16[32,4,8,2048]{3,2,1,0:T(8,128)(2,1)} copy(bf16[32,4,8,2048]{3,2,0,1:T(8,128)(2,1)} %convert_bitcast_fusion) | data formatting | bytes 8388608 | tf_op jit(solution)/shard_map/convert_element_type | solution.py:209
  309.5 7.7 %all-to-all-start.2 = ((bf16[32,4,8,2048]{3,2,1,0:T(8,128)(2,1)}), bf16[32,4,8,2048]{3,2,1,0:T(8,128)(2,1)}, u32[]{:S(2)}, u32[]{:S(2)}) async-start(bf16[32,4,8,2048]{3,2,1,0:T(8,128)(2,1)} %copy.211), calls=%async_computation.3 | async-start | bytes 8388608 | tf_op jit(solution)/shard_map/all_to_all | solution.py:206
  317.8 92.4 %all-to-all-done.2 = bf16[32,4,8,2048]{3,2,1,0:T(8,128)(2,1)} async-done(((bf16[32,4,8,2048]{3,2,1,0:T(8,128)(2,1)}), bf16[32,4,8,2048]{3,2,1,0:T(8,128)(2,1)}, u32[]{:S(2)}, u32[]{:S(2)}) %all-to-all-start.2) | async-done | bytes 4194336 | tf_op jit(solution)/shard_map/all_to_all | solution.py:206
  410.2 6.5 %bitcast_convert_fusion = f32[1024,2048]{1,0:T(8,128)} fusion(bf16[32,4,8,2048]{3,2,1,0:T(8,128)(2,1)} %all-to-all-done.2), kind=kLoop, calls=%fused_computation.11 | loop fusion | flops 2097152 | bytes 12582912 | tf_op jit(solution)/shard_map/reshape | solution.py:215
  416.7 8.9 %gather_fusion = f32[512,2048]{1,0:T(8,128)} fusion(f32[1024,2048]{1,0:T(8,128)} %bitcast_convert_fusion, s32[1024]{0:T(1024)S(1)} %pad_clamp_fusion), kind=kCustom, calls=%fused_computation | custom fusion | bytes 8390656 | tf_op jit(solution)/shard_map/gather | solution.py:216
  425.6 4.3 fusion.3
  429.9 31.6 %reduce-scatter.5.cloned.1.call-done = bf16[8,2048]{1,0:T(8,128)(2,1)} async-done(((bf16[64,2048]{1,0:T(8,128)(2,1)}), bf16[8,2048]{1,0:T(8,128)(2,1)}) %reduce-scatter.5.cloned.1.call-update) | async-done | bytes 32784 | tf_op jit(solution)/shard_map/reduce_scatter | solution.py:217
  461.5 1.4 fusion.85
  (134 shorter events, 6.8 us)
Async XLA Ops:
  7.2 134.0 %copy-start = (bf16[512,2048]{1,0:T(8,128)(2,1)S(1)}, bf16[512,2048]{1,0:T(8,128)(2,1)}, u32[]{:S(2)}) copy-start(bf16[512,2048]{1,0:T(8,128)(2,1)} %param.26) | copy-start | bytes 6291460
  7.2 20.3 %copy-start.15 = (f32[128]{0:T(128)S(1)}, f32[128]{0:T(128)}, u32[]{:S(2)}) copy-start(f32[128]{0:T(128)} %param.25) | copy-start | bytes 1540
  7.2 19.7 %copy-start.16 = (f32[128]{0:T(128)S(1)}, f32[128]{0:T(128)}, u32[]{:S(2)}) copy-start(f32[128]{0:T(128)} %param.24) | copy-start | bytes 1540
  7.2 20.0 %copy-start.18 = (s32[2]{0:T(128)S(1)}, s32[2]{0:T(128)}, u32[]{:S(2)}) copy-start(s32[2]{0:T(128)} %param.35) | copy-start | bytes 28
  7.2 20.0 %copy-start.17 = (s32[64]{0:T(128)S(1)}, s32[64]{0:T(128)}, u32[]{:S(2)}) copy-start(s32[64]{0:T(128)} %param.37) | copy-start | bytes 772
  7.2 20.1 %copy-start.19 = (s32[64]{0:T(128)S(1)}, s32[64]{0:T(128)}, u32[]{:S(2)}) copy-start(s32[64]{0:T(128)} %param.36) | copy-start | bytes 772
  7.2 112.3 %all-gather.2.cloned.1.call-start = ((), (), s32[]{:S(2)}) async-start(), calls=%async_computation.5 | async-start | bytes 9437184 | tf_op jit(solution)/shard_map/all_gather | solution.py:13
  27.7 13.7 %copy-start.10 = (bf16[64,128]{1,0:T(8,128)(2,1)}, bf16[64,128]{1,0:T(8,128)(2,1)S(1)}, u32[]{:S(2)}) copy-start(bf16[64,128]{1,0:T(8,128)(2,1)S(1)} %get-tuple-element.258) | copy-start | bytes 49156
  42.5 13.3 %copy-start.8 = (f32[64,4,1,8]{0,3,1,2:T(8,128)}, f32[64,4,1,8]{0,3,1,2:T(8,128)S(1)}, u32[]{:S(2)}) copy-start(f32[64,4,1,8]{0,3,1,2:T(8,128)S(1)} %copy.216) | copy-start | bytes 24580
  57.1 5.4 %copy-start.3 = (bf16[64,2,4,8,128]{4,3,2,1,0:T(8,128)(2,1)S(1)}, bf16[64,2,4,8,128]{4,3,2,1,0:T(8,128)(2,1)}, u32[]{:S(2)}) copy-start(bf16[64,2,4,8,128]{4,3,2,1,0:T(8,128)(2,1)} %get-tuple-element.247) | copy-start | bytes 3145732
  62.5 2.0 copy-start.12
  63.2 21.0 %copy-start.9 = (f32[64,4,1,8]{0,3,1,2:T(8,128)S(1)}, f32[64,4,1,8]{0,3,1,2:T(8,128)}, u32[]{:S(2)}) copy-start(f32[64,4,1,8]{0,3,1,2:T(8,128)} %copy-done.8) | copy-start | bytes 24580
  64.4 111.8 %reduce-scatter.3.cloned.1.call-start = ((), (), s32[]{:S(2)}) async-start(), calls=%async_computation.6 | async-start | bytes 294912 | tf_op jit(solution)/shard_map/reduce_scatter | solution.py:174
  78.9 0.7 copy-start.5
  97.7 0.7 copy-start.6
  140.9 35.3 %copy-start.4 = (bf16[8,2048]{1,0:T(8,128)(2,1)S(1)}, bf16[8,2048]{1,0:T(8,128)(2,1)}, u32[]{:S(2)}) copy-start(bf16[8,2048]{1,0:T(8,128)(2,1)} %param.20) | copy-start | bytes 98308
  140.9 41.1 %copy-start.13 = (s32[64,8]{0,1:T(8,128)S(1)}, s32[64,8]{0,1:T(8,128)}, u32[]{:S(2)}) copy-start(s32[64,8]{0,1:T(8,128)} %param.31) | copy-start | bytes 6148
  141.0 36.1 %copy-start.14 = (f32[2048]{0:T(1024)S(1)}, f32[2048]{0:T(1024)}, u32[]{:S(2)}) copy-start(f32[2048]{0:T(1024)} %param.27) | copy-start | bytes 24580
  178.7 10.8 %all-to-all-start = ((bf16[8,8,2048]{2,1,0:T(8,128)(2,1)}), bf16[8,8,2048]{2,1,0:T(8,128)(2,1)S(1)}, u32[]{:S(2)}, u32[]{:S(2)}) async-start(bf16[8,8,2048]{2,1,0:T(8,128)(2,1)} %stack.2), calls=%async_computation.1 | async-start | bytes 524288 | tf_op jit(solution)/shard_map/all_to_all | solution.py:197
  190.8 105.4 %copy-start.20 = (bf16[4,2048,96]{1,2,0:T(8,128)(2,1)S(1)}, bf16[4,2048,96]{1,2,0:T(8,128)(2,1)}, u32[]{:S(2)}) copy-start(bf16[4,2048,96]{1,2,0:T(8,128)(2,1)} %param.28) | copy-start | bytes 4718596
  294.2 2.0 copy-start.2
  309.5 8.1 %copy-start.11 = (f32[64,8]{0,1:T(8,128)S(1)}, f32[64,8]{0,1:T(8,128)}, u32[]{:S(2)}) copy-start(f32[64,8]{0,1:T(8,128)} %param.32) | copy-start | bytes 6148
  309.5 100.6 %all-to-all-start.2 = ((bf16[32,4,8,2048]{3,2,1,0:T(8,128)(2,1)}), bf16[32,4,8,2048]{3,2,1,0:T(8,128)(2,1)}, u32[]{:S(2)}, u32[]{:S(2)}) async-start(bf16[32,4,8,2048]{3,2,1,0:T(8,128)(2,1)} %copy.211), calls=%async_computation.3 | async-start | bytes 8388608 | tf_op jit(solution)/shard_map/all_to_all | solution.py:206
  317.2 144.3 %reduce-scatter.5.cloned.1.call-start = ((), (), s32[]{:S(2)}) async-start(), calls=%async_computation.7 | async-start | bytes 294912 | tf_op jit(solution)/shard_map/reduce_scatter | solution.py:217
  416.7 46.3 %copy-start.1 = (bf16[512,2048]{1,0:T(8,128)(2,1)S(1)}, bf16[512,2048]{1,0:T(8,128)(2,1)}, u32[]{:S(2)}) copy-start(bf16[512,2048]{1,0:T(8,128)(2,1)} %param.26) | copy-start | bytes 6291460
  425.6 36.0 %copy-start.7 = (bf16[8,2048]{1,0:T(8,128)(2,1)S(1)}, bf16[8,2048]{1,0:T(8,128)(2,1)}, u32[]{:S(2)}) copy-start(bf16[8,2048]{1,0:T(8,128)(2,1)} %reduce-scatter.3.cloned.1.call-done) | copy-start | bytes 98308
Sparse Core Ops, SparseCore 0:
  64.5 54.9 all-gather.1
  142.5 33.6 reduce-scatter.2
  430.1 31.4 reduce-scatter.4
